TPU v7x, 256 devices: a whole 4x4x8 slice. The times are simulated.
256 devices in a mesh: dp: 2 (over y_hi), retr: 16 (over x, y_lo, core), tensor: 8 (over z).
Axes of the slice: x: 4, y: 4 (y_hi: 2, y_lo: 2; y = y_hi * 2 + y_lo), z: 8, core: 2. Of those that a mesh axis runs over, the one named last changes fastest.
Arguments:
- hidden_in: bfloat16 [16384, 4096], P(('dp', 'retr'), 'tensor'), may hold values from -12 to 12
- norm_gain: float32 [4096], replicated, may hold values from 0.1 to 1.9
- nbr_table: int32 [256, 2], P(('dp', 'retr')), may hold values from 0 to 63, as said below
- encodings: bfloat16 [64, 128, 1024], P('retr'), may hold values from -21 to 21
- enc_mask: int32 [64, 4], P('retr'), may hold values from 0 to 1, as said below
- w_query: bfloat16 [4096, 4096], P(None, 'tensor'), may hold values from -0.02703125 to 0.02703125
- w_key: bfloat16 [1024, 4096], P(None, 'tensor'), may hold values from -0.1021875 to 0.1021875
- w_value: bfloat16 [1024, 4096], P(None, 'tensor'), may hold values from -0.1875 to 0.1875
- w_out: bfloat16 [4096, 4096], P('tensor'), may hold values from -0.125 to 0.125
Outputs:
- mixed: bfloat16 [16384, 4096], P(('dp', 'retr'), 'tensor')
Inputs may be any that keep to these rules, and one draw needn't show every extreme that they name: `nbr_table`: each aligned block of 8 table rows (the rows of one device) holds 16 distinct ids; at most 2 of them share the value id // 4, and in every block some value of id // 4 has exactly 2. `enc_mask`: in each row the ones come first; the first entry is 1.
All inputs are finite; a program needn't handle non-finite values.
Results may differ from a plain program's by a relative error of at most 0.012.
The roundings to bfloat16 on the way count: a program that leaves them out, or rounds other values in their place, can miss the bound.
Values may be sent and summed in bfloat16 or wider, within the bound.
No kernel may reach another device: no remote copies, remote signals or barrier semaphores. Data moves between devices by JAX's collectives and lax.ppermute only.
A program may use at most 128 MiB of HBM per device.

v0:
```python
import math
import jax
import jax.numpy as jnp
from jax import lax
from jax.sharding import PartitionSpec as P

HD = 128
NBRS = 2
BLOCK = 32


def attend_gathered(queries, key_value, selected_marks, segment_count, head_cols):
    tok_rows = queries.shape[0]
    head_count = head_cols // HD
    entry_keys = key_value.shape[0] // segment_count * key_value.shape[1]
    mask_cols = selected_marks.shape[1]
    key_block = key_value[:, :, :head_cols].reshape(segment_count, entry_keys, head_count, HD)
    value_block = key_value[:, :, head_cols:].reshape(segment_count, entry_keys, head_count, HD)
    key_live = (
        jnp.repeat(selected_marks.reshape(segment_count, NBRS * mask_cols), BLOCK, axis=1) > 0
    )
    query_block = queries.reshape(segment_count, tok_rows // segment_count, head_count, HD)
    factor = 1.0 / math.sqrt(HD)
    scores = (
        jnp.einsum("cqhd,ckhd->chqk", query_block, key_block, preferred_element_type=jnp.float32)
        * factor
    )
    key_open = key_live[:, None, None, :]
    scores = jnp.where(key_open, scores, -1e30)
    row_max = jnp.max(scores, axis=-1, keepdims=True)
    weights = jnp.exp(scores - row_max) * key_open.astype(jnp.float32)
    probabilities = (weights / jnp.sum(weights, axis=-1, keepdims=True)).astype(jnp.bfloat16)
    attended = jnp.einsum(
        "chqk,ckhd->cqhd", probabilities, value_block, preferred_element_type=jnp.float32
    )
    return attended.astype(jnp.bfloat16).reshape(tok_rows, head_cols)


def local(hidden_in, norm_gain, nbr_table, encodings, enc_mask, w_query, w_key, w_value, w_out):
    gathered = lax.all_gather(hidden_in, "tensor", axis=1, tiled=True)
    widened = gathered.astype(jnp.float32)
    mean_sq = jnp.mean(widened * widened, axis=-1, keepdims=True)
    normed = (widened * lax.rsqrt(mean_sq + 1e-05) * norm_gain).astype(jnp.bfloat16)
    queries = jnp.dot(normed, w_query, preferred_element_type=jnp.float32).astype(jnp.bfloat16)
    w_both = jnp.concatenate([w_key, w_value], axis=1)
    segment_count = nbr_table.shape[0]
    entry_len = encodings.shape[1]
    enc_width = encodings.shape[2]
    head_cols = w_key.shape[1]
    wanted = nbr_table.reshape(-1)
    need_count = wanted.shape[0]
    live_marks = enc_mask.astype(jnp.bfloat16)
    entry_rows = lax.all_gather(encodings, "retr", axis=0, tiled=True)
    entry_marks = lax.all_gather(live_marks, "retr", axis=0, tiled=True)
    piece_count = entry_rows.shape[0]
    one_hot = (wanted[:, None] == jnp.arange(piece_count, dtype=jnp.int32)[None, :]).astype(
        jnp.bfloat16
    )
    picked = jnp.einsum(
        "jn,nre->jre", one_hot, entry_rows, preferred_element_type=jnp.float32
    ).astype(jnp.bfloat16)
    picked_marks = jnp.dot(one_hot, entry_marks, preferred_element_type=jnp.float32).astype(
        jnp.bfloat16
    )
    key_value = jnp.dot(
        picked.reshape(need_count * entry_len, enc_width),
        w_both,
        preferred_element_type=jnp.float32,
    )
    key_value = key_value.astype(jnp.bfloat16).reshape(need_count, entry_len, 2 * head_cols)
    attended = attend_gathered(queries, key_value, picked_marks, segment_count, head_cols)
    partial_value = jnp.dot(attended, w_out, preferred_element_type=jnp.float32)
    summed = lax.psum_scatter(partial_value, "tensor", scatter_dimension=1, tiled=True)
    return (hidden_in.astype(jnp.float32) + summed).astype(jnp.bfloat16)


def solution(mesh):
    in_specs = (
        P(("dp", "retr"), "tensor"),
        P(),
        P(("dp", "retr"), None),
        P("retr", None, None),
        P("retr", None),
        P(None, "tensor"),
        P(None, "tensor"),
        P(None, "tensor"),
        P("tensor", None),
    )
    out_specs = P(("dp", "retr"), "tensor")
    return jax.shard_map(local, mesh=mesh, in_specs=in_specs, out_specs=out_specs, check_vma=False)
```

profile of v0, /device:TPU:1, one launch (start us, length us, event | category | flops | bytes accessed | tf_op | source)
XLA Modules:
  0.0 318.5 jit_solution(9526612523659051779)
XLA Ops:
  6.5 0.0 copy-start.6
  6.5 0.0 all-gather.6.cloned.1.call-start
  6.5 0.7 all-gather.6.cloned.1.call-update
  7.3 0.0 all-gather.4.cloned.1.call-start
  7.3 0.7 all-gather.4.cloned.1.call-update
  8.0 0.0 reduce-scatter.2.cloned.1.call-start
  8.1 0.8 copy.24
  8.8 0.1 eq.15
  8.9 0.7 convert_bitcast_fusion
  9.6 21.0 %all-gather = bf16[16,4,4]{2,1,0:T(4,128)(2,1)S(1)} all-gather(bf16[1,4,4]{2,1,0:T(4,128)(2,1)S(1)} %convert_bitcast_fusion), channel_id=1, replica_groups=mesh['dp'=2,'retr'=16,'tensor'=8] {'retr'}, dimensions={0}, use_global_device_ids=true | all-gather | bytes 544 | tf_op jit(solution)/shard_map/all_gather | solution.py:54
  30.6 0.2 fusion.30
  30.8 0.1 copy.28
  30.9 0.1 gt.22
  31.0 0.1 broadcast_in_dim.14
  31.0 0.1 gt.23
  31.2 36.4 %all-gather.6.cloned.1.call-done = bf16[512,4096]{1,0:T(8,128)(2,1)} async-done(((bf16[512,512]{1,0:T(8,128)(2,1)}), bf16[512,4096]{1,0:T(8,128)(2,1)}) %all-gather.6.cloned.1.call-update) | async-done | bytes 4194320 | tf_op jit(solution)/shard_map/all_gather | solution.py:40
  67.5 0.0 copy-start.1
  67.5 3.2 %fusion.3 = f32[512]{0:T(512)S(1)} fusion(bf16[512,4096]{1,0:T(8,128)(2,1)} %all-gather.6.cloned.1.call-done), kind=kLoop, calls=%fused_computation.5 | loop fusion | flops 6290944 | bytes 4196352 | tf_op jit(solution)/shard_map/reduce_sum | solution.py:42
  70.8 0.0 copy-done.6
  70.8 0.2 copy-done.1
  71.0 4.6 %fusion.24 = bf16[512,512]{1,0:T(8,128)(2,1)S(1)} fusion(bf16[4096,512]{1,0:T(8,128)(2,1)} %param.14, bf16[512,4096]{1,0:T(8,128)(2,1)S(1)} %copy-done.1, f32[4096]{0:T(1024)S(1)} %copy-done.6, f32[512]{0:T(512)S(1)} %add_rsqrt_fusion), kind=kOutput, calls=%fused_computation.25 | convolution fusion | flops 2156134400 | bytes 8931328 | tf_op jit(solution)/shard_map/dot_general | solution.py:44
  75.6 0.1 reshape.49
  75.7 87.0 %all-gather.4.cloned.1.call-done = bf16[64,128,1024]{2,1,0:T(8,128)(2,1)} async-done(((bf16[4,128,1024]{2,1,0:T(8,128)(2,1)}), bf16[64,128,1024]{2,1,0:T(8,128)(2,1)}) %all-gather.4.cloned.1.call-update) | async-done | bytes 16777232 | tf_op jit(solution)/shard_map/all_gather | solution.py:53
  162.7 23.7 %fusion.10 = bf16[16,128,1024]{2,0,1:T(8,128)(2,1)S(1)} fusion(bf16[64,128,1024]{2,1,0:T(8,128)(2,1)} %all-gather.4.cloned.1.call-done, s32[16]{0:T(128)S(1)} %eq.15), kind=kOutput, calls=%fused_computation.12 | convolution fusion | flops 270533632 | bytes 20971584 | tf_op jit(solution)/shard_map/jn,nre->jre/dot_general | solution.py:59
  186.4 0.0 copy-start.4
  186.4 0.0 copy-start.5
  186.4 2.5 copy.26
  188.9 0.0 copy-done.4
  189.0 0.0 copy-done.5
  189.0 5.0 %convolution_convert_fusion = bf16[2048,1024]{1,0:T(8,128)(2,1)S(1)} fusion(bf16[2048,1024]{1,0:T(8,128)(2,1)S(1)} %bitcast.20, bf16[1024,512]{1,0:T(8,128)(2,1)S(1)} %copy-done.4, bf16[1024,512]{1,0:T(8,128)(2,1)S(1)} %copy-done.5), kind=kOutput, calls=%fused_computation.11 | convolution fusion | flops 4301258752 | bytes 10485760 | tf_op jit(solution)/shard_map/dot_general | solution.py:65
  194.0 1.8 fusion.46
  195.8 4.0 %reshape.55 = bf16[8,256,4,128]{3,2,1,0:T(4,128)(2,1)} reshape(bf16[16,128,512]{2,1,0:T(8,128)(2,1)} %get-tuple-element.5) | data formatting | bytes 4194304 | tf_op jit(solution)/shard_map/reshape | solution.py:17
  199.8 2.0 reshape.56
  201.8 0.0 copy-start.2
  201.8 4.1 %fusion.47 = (f32[8,4,64]{2,1,0:T(4,128)S(1)}, f32[8,4,64,256]{3,2,1,0:T(8,128)}) fusion(f32[8,256]{1,0:T(8,128)S(1)} %convert_element_type.53, pred[8,256]{1,0:T(8,128)(4,1)S(1)} %gt.23, bf16[8,256,4,128]{3,2,1,0:T(4,128)(2,1)} %reshape.55, bf16[8,64,4,128]{3,2,1,0:T(4,128)(2,1)S(1)} %reshape.49), kind=kOutput, calls=%fused_computation.48 | convolution fusion | flops 136839424 | bytes 4737024 | tf_op jit(solution)/shard_map/sub | solution.py:31
  206.0 0.0 copy-done.2
  206.0 0.0 copy-start
  206.0 2.3 fusion.27
  208.3 0.4 copy.33
  208.7 0.1 copy-done
  208.8 5.6 %fusion.35 = f32[512,4096]{1,0:T(8,128)} fusion(bf16[512,4096]{1,0:T(8,128)(2,1)S(1)} %copy-done, bf16[64,8,4,128]{3,2,1,0:T(4,128)(2,1)S(1)} %bitcast.21), kind=kOutput, calls=%fused_computation.34 | convolution fusion | flops 2147483648 | bytes 13107200 | tf_op jit(solution)/shard_map/dot_general | solution.py:72
  214.4 0.0 copy-start.3
  214.4 0.0 reduce-scatter.2.cloned.1.call-update
  214.4 95.4 %reduce-scatter.2.cloned.1.call-done = f32[512,512]{1,0:T(8,128)} async-done(((f32[512,4096]{1,0:T(8,128)}), f32[512,512]{1,0:T(8,128)}) %reduce-scatter.2.cloned.1.call-update) | async-done | bytes 1048592 | tf_op jit(solution)/shard_map/reduce_scatter | solution.py:73
  309.8 0.0 copy-done.3
  309.8 2.2 add_convert_fusion
  (2 shorter events, 0.0 us)
Async XLA Ops:
  6.5 64.2 %copy-start.6 = (f32[4096]{0:T(1024)S(1)}, f32[4096]{0:T(1024)}, u32[]{:S(2)}) copy-start(f32[4096]{0:T(1024)} %param.10) | copy-start | bytes 49156
  6.5 61.0 %all-gather.6.cloned.1.call-start = ((), (), s32[]{:S(2)}) async-start(), calls=%async_computation.2 | async-start | bytes 4718592 | tf_op jit(solution)/shard_map/all_gather | solution.py:40
  7.3 155.4 %all-gather.4.cloned.1.call-start = ((), (), s32[]{:S(2)}) async-start(), calls=%async_computation.1 | async-start | bytes 17825792 | tf_op jit(solution)/shard_map/all_gather | solution.py:53
  8.0 301.8 %reduce-scatter.2.cloned.1.call-start = ((), (), s32[]{:S(2)}) async-start(), calls=%async_computation.3 | async-start | bytes 9437184 | tf_op jit(solution)/shard_map/reduce_scatter | solution.py:73
  67.5 3.4 %copy-start.1 = (bf16[512,4096]{1,0:T(8,128)(2,1)S(1)}, bf16[512,4096]{1,0:T(8,128)(2,1)}, u32[]{:S(2)}) copy-start(bf16[512,4096]{1,0:T(8,128)(2,1)} %all-gather.6.cloned.1.call-done) | copy-start | bytes 12582916
  186.4 2.6 copy-start.4
  186.4 2.6 copy-start.5
  201.8 4.2 %copy-start.2 = (bf16[8,256,4,128]{3,2,1,0:T(4,128)(2,1)S(1)}, bf16[8,256,4,128]{3,2,1,0:T(4,128)(2,1)}, u32[]{:S(2)}) copy-start(bf16[8,256,4,128]{3,2,1,0:T(4,128)(2,1)} %reshape.56) | copy-start | bytes 6291460
  206.0 2.8 copy-start
  214.4 95.4 %copy-start.3 = (bf16[512,512]{1,0:T(8,128)(2,1)S(1)}, bf16[512,512]{1,0:T(8,128)(2,1)}, u32[]{:S(2)}) copy-start(bf16[512,512]{1,0:T(8,128)(2,1)} %param.9) | copy-start | bytes 1572868
Sparse Core Ops, SparseCore 0:
  9.1 58.3 all-gather.5
  69.4 93.2 all-gather.3
  214.5 95.2 reduce-scatter.1
where the time goes:
time: 319 us
  waiting for transfers between devices  220 us (69%)
  matrix products  45.5 us (14%)
  blocking collectives  21 us (7%)
  between operations  13.2 us (4%)
  local copies, waits for them, and re-layouts  12.5 us (4%)
  other arithmetic  6.11 us (2%)
    reduce_scatter x1, waiting for transfers between devices, local(): lax.psum_scatter(partial_value, 'tensor', scatter_dimension=1, tiled=True)  95.4 us
    all_gather x1, waiting for transfers between devices, local(): entry_rows = lax.all_gather(encodings, 'retr', axis=0, tiled=True)  87 us
    all_gather x1, waiting for transfers between devices, local(): gathered = lax.all_gather(hidden_in, 'tensor', axis=1, tiled=True)  36.4 us
    dot_general x1, matrix products, local(): jnp.einsum('jn,nre->jre', one_hot, entry_rows, preferred_element_type=jnp...  23.7 us
    all_gather x1, blocking collectives, local(): entry_marks = lax.all_gather(live_marks, 'retr', axis=0, tiled=True)  21 us
  transfers between devices with their start and end apart: 3, of which 3 were waited for; matrix products, arithmetic and copies ran while one was open for 3% of the time, Pallas kernels for 0%

commit v1 on v0

--- a/solution.py
+++ b/solution.py
@@ -37,7 +37,9 @@
 
 
 def local(hidden_in, norm_gain, nbr_table, encodings, enc_mask, w_query, w_key, w_value, w_out):
-    gathered = lax.all_gather(hidden_in, "tensor", axis=1, tiled=True)
+    gathered = jnp.concatenate(
+        lax.all_to_all(jnp.stack([hidden_in] * lax.axis_size("tensor")), "tensor", 0, 0), axis=1
+    )
     widened = gathered.astype(jnp.float32)
     mean_sq = jnp.mean(widened * widened, axis=-1, keepdims=True)
     normed = (widened * lax.rsqrt(mean_sq + 1e-05) * norm_gain).astype(jnp.bfloat16)

time: 319 us -> 278 us (0.87)
  waiting for transfers between devices: 220 us -> 167 us
  starting transfers between devices: 0.08 us -> 9.18 us
    all_gather x1, waiting for transfers between devices: 87 us -> 0.02 us  [local(): entry_rows = lax.all_gather(encodings, 'retr', axis=0, tiled=True)]
    all_to_all x0 -> x1, waiting for transfers between devices: none -> 75.5 us  [local(): lax.all_to_all(jnp.stack([hidden_in] * lax.axis_size('tensor')), 'tensor'...]
    all_gather x1 -> x0, waiting for transfers between devices: 36.4 us -> none  [local(): gathered = lax.all_gather(hidden_in, 'tensor', axis=1, tiled=True)]
    all_to_all x0 -> x1, starting transfers between devices: none -> 9.13 us  [local(): lax.all_to_all(jnp.stack([hidden_in] * lax.axis_size('tensor')), 'tensor'...]
    reduce_scatter x1, waiting for transfers between devices: 95.4 us -> 91.2 us  [local(): lax.psum_scatter(partial_value, 'tensor', scatter_dimension=1, tiled=True)]
  transfers between devices with their start and end apart: 3 -> 3, of which waited for: 3 -> 2; matrix products, arithmetic and copies ran while one was open for 3% -> 5% of each run, Pallas kernels for 0% -> 0%
where the time goes in v1:
time: 278 us
  waiting for transfers between devices  167 us (60%)
  matrix products  43.6 us (16%)
  blocking collectives  20.5 us (7%)
  local copies, waits for them, and re-layouts  15.3 us (6%)
  between operations  13.5 us (5%)
  starting transfers between devices  9.18 us (3%)
  other arithmetic  8.45 us (3%)
    reduce_scatter x1, waiting for transfers between devices, local(): lax.psum_scatter(partial_value, 'tensor', scatter_dimension=1, tiled=True)  91.2 us
    all_to_all x1, waiting for transfers between devices, local(): lax.all_to_all(jnp.stack([hidden_in] * lax.axis_size('tensor')), 'tensor'...  75.5 us
    dot_general x1, matrix products, local(): jnp.einsum('jn,nre->jre', one_hot, entry_rows, preferred_element_type=jnp...  23.7 us
    all_gather x1, blocking collectives, local(): entry_marks = lax.all_gather(live_marks, 'retr', axis=0, tiled=True)  20.5 us
    all_to_all x1, starting transfers between devices, local(): lax.all_to_all(jnp.stack([hidden_in] * lax.axis_size('tensor')), 'tensor'...  9.13 us
    dot_general x1, matrix products, local(): partial_value = jnp.dot(attended, w_out, preferred_element_type=jnp.float32)  5.6 us
  transfers between devices with their start and end apart: 3, of which 2 were waited for; matrix products, arithmetic and copies ran while one was open for 5% of the time, Pallas kernels for 0%

profile of v1, /device:TPU:1, one launch (start us, length us, event | category | flops | bytes accessed | tf_op | source)
XLA Modules:
  0.0 278.0 jit_solution(12255420430768097233)
XLA Ops:
  6.5 0.0 all-gather.3.cloned.1.call-start
  6.5 0.7 all-gather.3.cloned.1.call-update
  7.3 1.3 copy.30
  8.5 2.3 stack.2
  10.9 0.0 copy-start.5
  10.9 0.0 copy-start.4
  10.9 9.1 %all-to-all-start = ((bf16[8,512,512]{1,2,0:T(8,128)(2,1)}), bf16[8,512,512]{1,2,0:T(8,128)(2,1)}, u32[]{:S(2)}, u32[]{:S(2)}) async-start(bf16[8,512,512]{1,2,0:T(8,128)(2,1)} %stack.2), calls=%async_computation | async-start | bytes 8388608 | tf_op jit(solution)/shard_map/all_to_all | solution.py:41
  20.0 0.0 copy-start.3
  20.0 0.0 reduce-scatter.2.cloned.1.call-start
  20.1 0.0 copy-done.5
  20.1 0.1 copy.25
  20.1 0.1 eq.15
  20.2 0.0 copy-done.4
  20.2 20.5 %all-gather = bf16[16,4,4]{2,1,0:T(4,128)(2,1)S(1)} all-gather(bf16[1,4,4]{2,1,0:T(4,128)(2,1)S(1)} %convert_bitcast_fusion), channel_id=1, replica_groups=mesh['dp'=2,'retr'=16,'tensor'=8] {'retr'}, dimensions={0}, use_global_device_ids=true | all-gather | bytes 544 | tf_op jit(solution)/shard_map/all_gather | solution.py:56
  40.8 0.2 fusion.22
  40.9 0.1 copy.29
  41.0 0.1 gt.22
  41.1 0.1 broadcast_in_dim.14
  41.2 0.1 gt.23
  41.3 75.5 %all-to-all-done = bf16[8,512,512]{1,2,0:T(8,128)(2,1)} async-done(((bf16[8,512,512]{1,2,0:T(8,128)(2,1)}), bf16[8,512,512]{1,2,0:T(8,128)(2,1)}, u32[]{:S(2)}, u32[]{:S(2)}) %all-to-all-start) | async-done | bytes 4194336 | tf_op jit(solution)/shard_map/all_to_all | solution.py:41
  116.8 3.1 %multiply_reduce_fusion = f32[512]{0:T(512)S(1)} fusion(bf16[8,512,512]{1,2,0:T(8,128)(2,1)} %all-to-all-done), kind=kLoop, calls=%fused_computation.6 | loop fusion | flops 6290944 | bytes 4196352 | tf_op jit(solution)/shard_map/reduce_sum | solution.py:44
  120.0 0.0 copy-done.3
  120.0 0.0 copy-start.6
  120.0 3.1 %fusion.4 = bf16[512,4096]{0,1:T(8,128)(2,1)S(1)} fusion(f32[4096]{0:T(1024)S(1)} %copy-done.3, f32[512]{0:T(512)S(1)} %add_rsqrt_fusion, bf16[8,512,512]{1,2,0:T(8,128)(2,1)} %all-to-all-done), kind=kLoop, calls=%fused_computation.5 | loop fusion | flops 8388608 | bytes 8407040 | tf_op jit(solution)/shard_map/convert_element_type | solution.py:45
  123.1 0.3 copy-done.6
  123.5 2.4 convolution_convert_fusion.1
  125.8 0.1 reshape.55
  126.0 0.0 all-gather.3.cloned.1.call-done
  126.0 23.7 %fusion.5 = bf16[16,128,1024]{2,0,1:T(8,128)(2,1)S(1)} fusion(bf16[64,128,1024]{2,1,0:T(8,128)(2,1)} %all-gather.3.cloned.1.call-done, s32[16]{0:T(128)S(1)} %eq.15), kind=kOutput, calls=%fused_computation.8 | convolution fusion | flops 270533632 | bytes 20971584 | tf_op jit(solution)/shard_map/jn,nre->jre/dot_general | solution.py:61
  149.7 0.0 copy-start.7
  149.7 2.3 copy.27
  152.1 0.0 copy-done.7
  152.1 0.0 copy-done.8
  152.1 5.3 %convolution_convert_fusion = bf16[2048,1024]{1,0:T(8,128)(2,1)S(1)} fusion(bf16[2048,1024]{1,0:T(8,128)(2,1)S(1)} %bitcast.29, bf16[1024,512]{1,0:T(8,128)(2,1)S(1)} %copy-done.7, bf16[1024,512]{1,0:T(8,128)(2,1)S(1)} %copy-done.8), kind=kOutput, calls=%fused_computation.7 | convolution fusion | flops 4301258752 | bytes 10485760 | tf_op jit(solution)/shard_map/dot_general | solution.py:67
  157.4 1.8 fusion.38
  159.2 4.0 %reshape.62 = bf16[8,256,4,128]{3,2,1,0:T(4,128)(2,1)} reshape(bf16[16,128,512]{2,1,0:T(8,128)(2,1)} %get-tuple-element.5) | data formatting | bytes 4194304 | tf_op jit(solution)/shard_map/reshape | solution.py:17
  163.1 2.0 reshape.63
  165.2 0.0 copy-start.1
  165.2 4.2 %fusion.39 = (f32[8,4,64]{2,1,0:T(4,128)S(1)}, f32[8,4,64,256]{3,2,1,0:T(8,128)}) fusion(f32[8,256]{1,0:T(8,128)S(1)} %convert_element_type.66, pred[8,256]{1,0:T(8,128)(4,1)S(1)} %gt.23, bf16[8,256,4,128]{3,2,1,0:T(4,128)(2,1)} %reshape.62, bf16[8,64,4,128]{3,2,1,0:T(4,128)(2,1)S(1)} %reshape.55), kind=kOutput, calls=%fused_computation.44 | convolution fusion | flops 136839424 | bytes 4737024 | tf_op jit(solution)/shard_map/sub | solution.py:31
  169.3 0.0 copy-done.1
  169.3 2.3 fusion.19
  171.6 0.4 copy.35
  172.0 0.1 copy-done
  172.2 5.6 %fusion.27 = f32[512,4096]{1,0:T(8,128)} fusion(bf16[512,4096]{1,0:T(8,128)(2,1)S(1)} %copy-done, bf16[64,8,4,128]{3,2,1,0:T(4,128)(2,1)S(1)} %bitcast.30), kind=kOutput, calls=%fused_computation.30 | convolution fusion | flops 2147483648 | bytes 13107200 | tf_op jit(solution)/shard_map/dot_general | solution.py:74
  177.8 0.0 reduce-scatter.2.cloned.1.call-update
  177.8 91.2 %reduce-scatter.2.cloned.1.call-done = f32[512,512]{1,0:T(8,128)} async-done(((f32[512,4096]{1,0:T(8,128)}), f32[512,512]{1,0:T(8,128)}) %reduce-scatter.2.cloned.1.call-update) | async-done | bytes 1048592 | tf_op jit(solution)/shard_map/reduce_scatter | solution.py:75
  269.0 0.0 copy-done.2
  269.0 2.2 add_convert_fusion
  (6 shorter events, 0.0 us)
Async XLA Ops:
  6.5 119.4 %all-gather.3.cloned.1.call-start = ((), (), s32[]{:S(2)}) async-start(), calls=%async_computation.2 | async-start | bytes 17825792 | tf_op jit(solution)/shard_map/all_gather | solution.py:55
  10.9 9.2 %copy-start.5 = (s32[8,2]{0,1:T(2,128)S(1)}, s32[8,2]{0,1:T(2,128)}, u32[]{:S(2)}) copy-start(s32[8,2]{0,1:T(2,128)} %param.11) | copy-start | bytes 196
  10.9 9.4 %copy-start.4 = (s32[4,4]{1,0:T(4,128)S(1)}, s32[4,4]{1,0:T(4,128)}, u32[]{:S(2)}) copy-start(s32[4,4]{1,0:T(4,128)} %param.13) | copy-start | bytes 196
  10.9 106.0 %all-to-all-start = ((bf16[8,512,512]{1,2,0:T(8,128)(2,1)}), bf16[8,512,512]{1,2,0:T(8,128)(2,1)}, u32[]{:S(2)}, u32[]{:S(2)}) async-start(bf16[8,512,512]{1,2,0:T(8,128)(2,1)} %stack.2), calls=%async_computation | async-start | bytes 8388608 | tf_op jit(solution)/shard_map/all_to_all | solution.py:41
  20.0 100.0 %copy-start.3 = (f32[4096]{0:T(1024)S(1)}, f32[4096]{0:T(1024)}, u32[]{:S(2)}) copy-start(f32[4096]{0:T(1024)} %param.10) | copy-start | bytes 49156
  20.0 249.0 %reduce-scatter.2.cloned.1.call-start = ((), (), s32[]{:S(2)}) async-start(), calls=%async_computation.3 | async-start | bytes 9437184 | tf_op jit(solution)/shard_map/reduce_scatter | solution.py:75
  120.0 3.5 %copy-start.6 = (bf16[4096,512]{1,0:T(8,128)(2,1)S(1)}, bf16[4096,512]{1,0:T(8,128)(2,1)}, u32[]{:S(2)}) copy-start(bf16[4096,512]{1,0:T(8,128)(2,1)} %param.14) | copy-start | bytes 12582916
  149.7 2.3 copy-start.7
  149.7 2.4 copy-start.8
  165.2 4.2 %copy-start.1 = (bf16[8,256,4,128]{3,2,1,0:T(4,128)(2,1)S(1)}, bf16[8,256,4,128]{3,2,1,0:T(4,128)(2,1)}, u32[]{:S(2)}) copy-start(bf16[8,256,4,128]{3,2,1,0:T(4,128)(2,1)} %reshape.63) | copy-start | bytes 6291460
  169.3 2.8 %copy-start = (bf16[512,4096]{1,0:T(8,128)(2,1)S(1)}, bf16[512,4096]{1,0:T(8,128)(2,1)}, u32[]{:S(2)}) copy-start(bf16[512,4096]{1,0:T(8,128)(2,1)} %param.17) | copy-start | bytes 12582916
  177.8 91.2 %copy-start.2 = (bf16[512,512]{1,0:T(8,128)(2,1)S(1)}, bf16[512,512]{1,0:T(8,128)(2,1)}, u32[]{:S(2)}) copy-start(bf16[512,512]{1,0:T(8,128)(2,1)} %param.9) | copy-start | bytes 1572868
Sparse Core Ops, SparseCore 0:
  9.2 98.3 all-gather.2
  177.9 91.0 reduce-scatter.1
